TPU v7x, 256 devices: a whole 4x4x8 slice. The times are simulated.
256 devices in a mesh: ctx: 32 (over y, x, core), head: 8 (over z).
Axes of the slice: x: 4, y: 4, z: 8, core: 2. Of those that a mesh axis runs over, the one named last changes fastest.
Arguments:
- query_vectors: bfloat16 [4096, 4096], P('ctx', 'head'), may hold values from -6 to 6
- key_vectors: bfloat16 [4096, 4096], P('ctx', 'head'), may hold values from -1.5 to 1.5
- value_vectors: bfloat16 [4096, 4096], P('ctx', 'head'), may hold values from -6 to 6
- log_decay: float32 [32, 4096], P('head', 'ctx'), may hold values from -2 to 0, as said below
- residual: bfloat16 [4096, 3072], P('ctx'), may hold values from -6 to 6
- out_weight: bfloat16 [4096, 3072], P('head', 'ctx'), may hold values from -0.09375 to 0.09375
- attn_gain: float32 [4096], P('head'), may hold values from 0.1 to 1.9
- moe_gain: float32 [3072], replicated, may hold values from 0.1 to 1.9
- router: float32 [3072, 32], replicated, may hold values from -0.109375 to 0.109375
- w_gate: bfloat16 [32, 3072, 4608], P('ctx', None, 'head'), may hold values from -0.109375 to 0.109375
- w_up: bfloat16 [32, 3072, 4608], P('ctx', None, 'head'), may hold values from -0.109375 to 0.109375
- w_down: bfloat16 [32, 4608, 3072], P('ctx', 'head'), may hold values from -0.09375 to 0.09375
- expert_ids: int32 [4096, 2], P('ctx'), may hold values from 0 to 31, all different within a row; in each aligned block of 128 rows (0 to 127, 128 to 255, ...) at most 16 rows name the same one
Outputs:
- final_out: bfloat16 [4096, 3072], P('ctx', 'head')
Inputs may be any that keep to these rules, and one draw needn't show every extreme that they name: `expert_ids`: each row names 2 different experts. In each aligned block of 128 rows no expert is named by more than 16 rows, and in every draw some expert is named by exactly 16 rows of some block. `log_decay`: every entry is negative.
All inputs are finite; a program needn't handle non-finite values.
Results may differ from a plain program's by a relative error of at most 0.022.
Values may be sent and summed in bfloat16 or wider, within the bound.
No kernel may reach another device: no remote copies, remote signals or barrier semaphores. Data moves between devices by JAX's collectives and lax.ppermute only.
A program may use at most 128 MiB of HBM per device.

v0:
```python
import jax
import jax.numpy as jnp
from jax import lax
from jax.sharding import PartitionSpec as P

TOP = 2
PRECISE = lax.Precision.HIGHEST


def prior_states(final_log, local_state, axis):
    index = lax.axis_index(axis)
    totals = lax.all_gather(final_log, axis)
    states = lax.all_gather(local_state.astype(jnp.bfloat16), axis)
    peers = totals.shape[0]
    source = lax.broadcasted_iota(jnp.int32, (peers, peers), 0)
    between = lax.broadcasted_iota(jnp.int32, (peers, peers), 1)
    inside = (between > source) & (between < index)
    spans = jnp.sum(jnp.where(inside[:, :, None], totals[None, :, :], 0.0), axis=1)
    weights = jnp.where(jnp.arange(peers)[:, None] < index, jnp.exp(spans), 0.0)
    return jnp.einsum("jh,jhde->hde", weights, states.astype(jnp.float32), precision=PRECISE)


def local_attention(query_block, key_block, value_block, decay_block):
    running = jnp.cumsum(decay_block, axis=1)
    length_here = decay_block.shape[1]
    row_index = lax.broadcasted_iota(jnp.int32, (length_here, length_here), 0)
    col_index = lax.broadcasted_iota(jnp.int32, (length_here, length_here), 1)
    causal = (col_index <= row_index)[None]
    spread = jnp.where(causal, running[:, :, None] - running[:, None, :], 0.0)
    decay_weights = jnp.where(causal, jnp.exp(spread), 0.0)
    scores = jnp.einsum("htd,hsd->hts", query_block, key_block, precision=PRECISE) * decay_weights
    inside_part = jnp.einsum("hts,hse->hte", scores, value_block, precision=PRECISE)
    final_log = running[:, -1]
    tail_decay = jnp.exp(final_log[:, None] - running)
    local_state = jnp.einsum(
        "hsd,hse->hde", key_block * tail_decay[:, :, None], value_block, precision=PRECISE
    )
    return (inside_part, running, local_state, final_log)


def route_tokens(logits, expert_ids, experts_total):
    onehot = expert_ids[:, :, None] == lax.broadcasted_iota(jnp.int32, (1, 1, experts_total), 2)
    chosen = jnp.sum(jnp.where(onehot, logits[:, None, :], 0.0), axis=2)
    leading = jax.nn.sigmoid(chosen[:, 0] - chosen[:, 1])
    gate_weights = jnp.stack([leading, 1.0 - leading], axis=1)
    marked = onehot.reshape(-1, experts_total).astype(jnp.int32)
    earlier = jnp.cumsum(marked, axis=0) - marked
    slot_index = jnp.sum(earlier * marked, axis=1).reshape(expert_ids.shape)
    return (gate_weights, slot_index)


def body(
    query_vectors,
    key_vectors,
    value_vectors,
    log_decay,
    residual,
    out_weight,
    attn_gain,
    moe_gain,
    router,
    w_gate,
    w_up,
    w_down,
    expert_ids,
):
    token_count = query_vectors.shape[0]
    heads_here = log_decay.shape[0]
    head_size = query_vectors.shape[1] // heads_here

    def split_heads(matrix_in):
        return (
            matrix_in.astype(jnp.float32)
            .reshape(token_count, heads_here, head_size)
            .transpose(1, 0, 2)
        )

    query_heads = split_heads(query_vectors)
    inside_part, running, local_state, final_log = local_attention(
        query_heads, split_heads(key_vectors), split_heads(value_vectors), log_decay
    )
    prior_state = prior_states(final_log, local_state, "ctx")
    outside_part = jnp.exp(running)[:, :, None] * jnp.einsum(
        "htd,hde->hte", query_heads, prior_state, precision=PRECISE
    )
    attended = inside_part + outside_part
    square_mean = jnp.mean(attended * attended, axis=2, keepdims=True)
    heads_normed = (
        attended * lax.rsqrt(square_mean + 1e-05) * attn_gain.reshape(heads_here, 1, head_size)
    )
    heads_normed = (
        heads_normed.astype(jnp.bfloat16)
        .transpose(1, 0, 2)
        .reshape(token_count, heads_here * head_size)
    )
    partial_out = jnp.dot(
        heads_normed,
        lax.all_gather(out_weight, "ctx", axis=1, tiled=True),
        preferred_element_type=jnp.float32,
    )
    model_width = residual.shape[1]
    experts_total = router.shape[1]
    capacity = 2 * token_count * TOP // experts_total
    slice_width = model_width // lax.axis_size("head")
    slice_start = lax.axis_index("head") * slice_width
    projected = lax.psum(partial_out.astype(jnp.bfloat16), "head").astype(jnp.float32)
    mixed_rows = (residual.astype(jnp.float32) + projected).astype(jnp.bfloat16)
    mixed_wide = mixed_rows.astype(jnp.float32)
    inv_rms = lax.rsqrt(jnp.mean(mixed_wide * mixed_wide, axis=1, keepdims=True) + 1e-06)
    scaled = mixed_wide * moe_gain[None, :]
    moe_in = (scaled * inv_rms).astype(jnp.bfloat16)
    logits = inv_rms * jnp.dot(scaled, router, precision=PRECISE)
    base_slice = lax.dynamic_slice_in_dim(mixed_wide, slice_start, slice_width, 1)
    gate_weights, slot_index = route_tokens(logits, expert_ids, experts_total)
    target = (expert_ids * capacity + slot_index).reshape(-1)
    width_here = moe_in.shape[1]
    source = jnp.repeat(moe_in, TOP, axis=0)
    packed = jnp.zeros((experts_total * capacity, width_here), jnp.bfloat16).at[target].set(source)
    arrived = lax.all_to_all(
        packed.reshape(experts_total, capacity, width_here),
        "ctx",
        split_axis=0,
        concat_axis=0,
        tiled=True,
    )
    flat_rows = arrived.reshape(-1, model_width)
    gate_part = jnp.dot(flat_rows, w_gate[0], preferred_element_type=jnp.float32)
    up_part = jnp.dot(flat_rows, w_up[0], preferred_element_type=jnp.float32)
    hidden = (jax.nn.silu(gate_part) * up_part).astype(jnp.bfloat16)
    partial_down = jnp.dot(hidden, w_down[0], preferred_element_type=jnp.float32)
    summed = lax.psum_scatter(
        partial_down.astype(jnp.bfloat16), "head", scatter_dimension=1, tiled=True
    )
    returned = lax.all_to_all(
        summed.reshape(experts_total, capacity, slice_width),
        "ctx",
        split_axis=0,
        concat_axis=0,
        tiled=True,
    )
    lookup = returned.reshape(experts_total * capacity, slice_width)
    picked = lookup[target].reshape(token_count, TOP, slice_width).astype(jnp.float32)
    final_out = (
        base_slice + gate_weights[:, 0:1] * picked[:, 0] + gate_weights[:, 1:2] * picked[:, 1]
    )
    return final_out.astype(jnp.bfloat16)


def solution(mesh):
    in_specs = (
        P("ctx", "head"),
        P("ctx", "head"),
        P("ctx", "head"),
        P("head", "ctx"),
        P("ctx", None),
        P("head", "ctx"),
        P("head"),
        P(),
        P(),
        P("ctx", None, "head"),
        P("ctx", None, "head"),
        P("ctx", "head", None),
        P("ctx", None),
    )
    out_specs = P("ctx", "head")
    return jax.shard_map(body, mesh=mesh, in_specs=in_specs, out_specs=out_specs, check_vma=False)
```

profile of v0, /device:TPU:1, one launch (start us, length us, event | category | flops | bytes accessed | tf_op | source)
XLA Modules:
  0.0 356.7 jit_solution(9251623039175811909)
XLA Ops:
  6.5 1.1 reduce_window_sum.26
  7.7 0.2 slice_reduce_fusion.1
  7.9 0.6 exponential_bitcast_fusion
  8.5 1.7 copy.78
  10.1 1.9 convolution_convert_fusion.2
  12.0 0.0 all-gather.7.cloned.1.call-update
  12.0 0.0 all-gather.5.cloned.1.call-start
  12.1 0.7 all-gather.5.cloned.1.call-update
  12.8 0.0 all-reduce.3.cloned.1.call-start
  12.8 1.3 dynamic-slice
  14.7 0.2 dynamic-update-slice
  15.0 66.0 %all-reduce = f32[128]{0:T(128)} all-reduce(f32[128]{0:T(128)S(1)} %dynamic-update-slice), channel_id=2, replica_groups=mesh['ctx'=32,'head'=8] {'ctx'}, use_global_device_ids=true, to_apply=%add | all-reduce | flops 128 | bytes 1024
  81.0 0.7 reshape.188
  81.8 0.7 copy.65
  82.4 1.4 copy.66
  83.8 1.6 eq.39
  85.4 0.8 select_reduce_fusion
  86.2 1.9 convolution_multiply_fusion
  88.1 5.7 %fusion = f32[4,1,128,128]{3,1,2,0:T(1,128)S(1)} fusion(f32[32,4,1,1]{0,2,3,1:T(1,128)S(1)} %bitcast.151, bf16[32,4,128,128]{3,2,1,0:T(8,128)(2,1)} %bitcast.142), kind=kOutput, calls=%fused_computation.3 | convolution fusion | flops 25165824 | bytes 4456960 | tf_op jit(solution)/shard_map/jh,jhde->hde/dot_general | solution.py:20
  93.9 0.4 fusion.39
  94.3 0.4 fusion.26
  94.8 0.8 fusion.30
  95.6 23.6 %all-gather.5.cloned.1.call-done = bf16[512,3072]{0,1:T(8,128)(2,1)} async-done(((bf16[512,96]{0,1:T(8,128)(2,1)}), bf16[512,3072]{0,1:T(8,128)(2,1)}) %all-gather.5.cloned.1.call-update) | async-done | bytes 3145744 | tf_op jit(solution)/shard_map/all_gather | solution.py:98
  119.2 4.0 %convolution_convert_fusion.1 = bf16[128,3072]{1,0:T(8,128)(2,1)} fusion(bf16[128,512]{0,1:T(8,128)(2,1)} %bitcast.147, bf16[512,3072]{0,1:T(8,128)(2,1)} %all-gather.5.cloned.1.call-done), kind=kOutput, calls=%fused_computation.5 | convolution fusion | flops 403046400 | bytes 4063232 | tf_op jit(solution)/shard_map/dot_general | solution.py:96
  123.2 0.0 all-reduce.3.cloned.1.call-update
  123.3 0.2 reduce-scatter.4.cloned.1.call-start
  123.5 1.3 fusion.48
  124.8 1.5 eq.35
  126.3 1.9 reduce-window.6
  128.2 1.5 slice_reduce_fusion
  129.7 1.3 reduce-window.9
  131.0 0.7 slice.28
  131.6 1.4 fusion.47
  133.1 1.4 reshape.164
  134.5 1.5 copy.69
  136.0 1.2 multiply_add_fusion
  137.2 1.4 copy.70
  138.6 1.5 reshape.165
  140.1 1.2 compare_select_fusion
  141.3 51.4 %all-reduce.3.cloned.1.call-done = bf16[128,3072]{1,0:T(8,128)(2,1)} async-done(((bf16[128,3072]{1,0:T(8,128)(2,1)}), bf16[128,3072]{1,0:T(8,128)(2,1)}) %all-reduce.3.cloned.1.call-update) | async-done | bytes 786448 | tf_op jit(solution)/shard_map/psum | solution.py:106
  192.7 2.7 fusion.51
  195.4 0.2 multiply_reduce_fusion
  195.6 0.7 copy-done.1
  196.3 0.5 copy-done.12
  196.9 0.2 multiply_convert_fusion
  197.1 2.0 broadcast_in_dim.93
  199.1 4.6 %reshape.184 = bf16[256,3072]{1,0:T(8,128)(2,1)} reshape(bf16[128,2,3072]{2,1,0:T(2,128)(2,1)} %broadcast_in_dim.93) | data formatting | bytes 3145728 | tf_op jit(solution)/shard_map/reshape | solution.py:117
  203.7 5.8 %scatter_custom_fusion = bf16[512,3072]{1,0:T(8,128)(2,1)} fusion(s32[256]{0:T(256)} %bitcast.152, bf16[256,3072]{1,0:T(8,128)(2,1)} %reshape.184, bf16[]{:T(256)} %constant.42.clone.1), kind=kCustom, calls=%fused_computation.12 | custom fusion | bytes 3146240 | tf_op jit(solution)/shard_map/scatter | solution.py:118
  209.4 51.8 %all_to_all.10 = bf16[32,16,3072]{2,1,0:T(8,128)(2,1)S(1)} all-to-all(bf16[32,16,3072]{2,1,0:T(8,128)(2,1)} %bitcast.141), channel_id=1, replica_groups=mesh['ctx'=32,'head'=8] {'ctx'}, dimensions={0} | all-to-all | bytes 6291456 | tf_op jit(solution)/shard_map/all_to_all | solution.py:119
  261.2 1.7 copy-done.2
  262.9 3.1 fusion.5
  266.1 9.5 %convolution_convert_fusion = bf16[512,3072]{1,0:T(8,128)(2,1)} fusion(bf16[1,576,3072]{2,1,0:T(8,128)(2,1)S(1)} %copy-done, bf16[512,3072]{1,0:T(8,128)(2,1)} %bitcast.144, bf16[1,3072,576]{1,2,0:T(8,128)(2,1)} %param.23, f32[512,576]{0,1:T(8,128)} %fusion.5), kind=kOutput, calls=%fused_computation.2 | convolution fusion | flops 3627220992 | bytes 14548992 | tf_op jit(solution)/shard_map/dot_general | solution.py:130
  275.6 4.7 %copy.81 = bf16[512,3072]{0,1:T(8,128)(2,1)} copy(bf16[512,3072]{1,0:T(8,128)(2,1)} %convolution_convert_fusion) | data formatting | bytes 6291456
  280.3 0.0 reduce-scatter.4.cloned.1.call-update
  280.3 1.2 pad_clamp_fusion
  281.5 37.5 %reduce-scatter.4.cloned.1.call-done = bf16[384,512]{1,0:T(8,128)(2,1)} async-done(((bf16[3072,512]{1,0:T(8,128)(2,1)}), bf16[384,512]{1,0:T(8,128)(2,1)}) %reduce-scatter.4.cloned.1.call-update) | async-done | bytes 393232
  319.0 2.0 copy.82
  321.0 11.0 %all-to-all-start.1 = ((bf16[32,16,384]{2,1,0:T(8,128)(2,1)}), bf16[32,16,384]{2,1,0:T(8,128)(2,1)}, u32[]{:S(2)}, u32[]{:S(2)}) async-start(bf16[32,16,384]{2,1,0:T(8,128)(2,1)} %bitcast.145), calls=%async_computation.1 | async-start | bytes 786432 | tf_op jit(solution)/shard_map/all_to_all | solution.py:134
  332.0 2.8 fusion.18
  334.8 7.4 %all-to-all-done.1 = bf16[32,16,384]{2,1,0:T(8,128)(2,1)} async-done(((bf16[32,16,384]{2,1,0:T(8,128)(2,1)}), bf16[32,16,384]{2,1,0:T(8,128)(2,1)}, u32[]{:S(2)}, u32[]{:S(2)}) %all-to-all-start.1) | async-done | bytes 393248 | tf_op jit(solution)/shard_map/all_to_all | solution.py:134
  342.2 3.0 gather_fusion
  345.2 1.9 reshape.171
  347.0 1.5 fusion.52
  348.5 1.7 fusion.35
  (36 shorter events, 0.1 us)
Async XLA Ops:
  6.5 259.6 %copy-start = (bf16[1,576,3072]{2,1,0:T(8,128)(2,1)S(1)}, bf16[1,576,3072]{2,1,0:T(8,128)(2,1)}, u32[]{:S(2)}) copy-start(bf16[1,576,3072]{2,1,0:T(8,128)(2,1)} %param.24) | copy-start | bytes 10616836
  6.5 81.6 %all-gather.7.cloned.1.call-start = ((), (), s32[]{:S(2)}) async-start(), calls=%async_computation.5 | async-start | bytes 4325376 | tf_op jit(solution)/shard_map/all_gather | solution.py:13
  7.7 7.3 %copy-start.7 = (f32[4,128]{1,0:T(4,128)}, f32[4,128]{1,0:T(4,128)S(1)}, u32[]{:S(2)}) copy-start(f32[4,128]{1,0:T(4,128)S(1)} %reduce_window_sum.26) | copy-start | bytes 6148
  12.0 107.2 %all-gather.5.cloned.1.call-start = ((), (), s32[]{:S(2)}) async-start(), calls=%async_computation.3 | async-start | bytes 3244032 | tf_op jit(solution)/shard_map/all_gather | solution.py:98
  12.8 179.9 %all-reduce.3.cloned.1.call-start = ((), (), s32[]{:S(2)}) async-start(), calls=%async_computation.4 | async-start | bytes 1572864 | tf_op jit(solution)/shard_map/psum | solution.py:106
  82.4 11.8 %copy-start.10 = (f32[4,128]{1,0:T(4,128)S(1)}, f32[4,128]{1,0:T(4,128)}, u32[]{:S(2)}) copy-start(f32[4,128]{1,0:T(4,128)} %get-tuple-element.12) | copy-start | bytes 6148
  88.1 6.7 %copy-start.9 = (f32[128,4]{0,1:T(4,128)S(1)}, f32[128,4]{0,1:T(4,128)}, u32[]{:S(2)}) copy-start(f32[128,4]{0,1:T(4,128)} %get-tuple-element.11) | copy-start | bytes 6148
  88.1 5.8 %copy-start.5 = (bf16[128,512]{1,0:T(8,128)(2,1)S(1)}, bf16[128,512]{1,0:T(8,128)(2,1)}, u32[]{:S(2)}) copy-start(bf16[128,512]{1,0:T(8,128)(2,1)} %param.13) | copy-start | bytes 393220
  88.1 6.2 %copy-start.3 = (bf16[128,512]{1,0:T(8,128)(2,1)S(1)}, bf16[128,512]{1,0:T(8,128)(2,1)}, u32[]{:S(2)}) copy-start(bf16[128,512]{1,0:T(8,128)(2,1)} %param.15) | copy-start | bytes 393220
  88.1 6.2 %copy-start.4 = (f32[4,128,128]{2,1,0:T(8,128)S(1)}, f32[4,128,128]{2,1,0:T(8,128)}, u32[]{:S(2)}) copy-start(f32[4,128,128]{2,1,0:T(8,128)} %convolution_multiply_fusion) | copy-start | bytes 786436
  88.1 6.7 %copy-start.11 = (f32[512]{0:T(512)S(1)}, f32[512]{0:T(512)}, u32[]{:S(2)}) copy-start(f32[512]{0:T(512)} %param.19) | copy-start | bytes 6148
  94.8 41.2 %copy-start.8 = (s32[128,2]{0,1:T(2,128)S(1)}, s32[128,2]{0,1:T(2,128)}, u32[]{:S(2)}) copy-start(s32[128,2]{0,1:T(2,128)} %param.25) | copy-start | bytes 3076
  123.2 73.6 %copy-start.6 = (f32[3072]{0:T(1024)S(1)}, f32[3072]{0:T(1024)}, u32[]{:S(2)}) copy-start(f32[3072]{0:T(1024)} %param.20) | copy-start | bytes 36868
  123.3 195.8 %reduce-scatter.4.cloned.1.call-start = ((), (), s32[]{:S(2)}) async-start(), calls=%async_computation.6 | async-start | bytes 3538944
  195.4 0.9 copy-start.1
  196.3 0.5 copy-start.12
  209.4 53.5 %copy-start.13 = (bf16[1,3072,576]{1,2,0:T(8,128)(2,1)S(1)}, bf16[1,3072,576]{1,2,0:T(8,128)(2,1)}, u32[]{:S(2)}) copy-start(bf16[1,3072,576]{1,2,0:T(8,128)(2,1)} %param.22) | copy-start | bytes 10616836
  261.2 1.7 copy-start.2
  321.0 21.2 %all-to-all-start.1 = ((bf16[32,16,384]{2,1,0:T(8,128)(2,1)}), bf16[32,16,384]{2,1,0:T(8,128)(2,1)}, u32[]{:S(2)}, u32[]{:S(2)}) async-start(bf16[32,16,384]{2,1,0:T(8,128)(2,1)} %bitcast.145), calls=%async_computation.1 | async-start | bytes 786432 | tf_op jit(solution)/shard_map/all_to_all | solution.py:134
Sparse Core Ops, SparseCore 0:
  12.1 55.2 all-gather.6
  70.0 49.2 all-gather.4
  123.4 69.2 all-reduce.2
  280.4 38.5 reduce-scatter.3
where the time goes:
time: 358 us; the launch traced here: 357 us
  waiting for transfers between devices  121 us (34%)
  blocking collectives  118 us (33%)
  local copies, waits for them, and re-layouts  45.6 us (13%)
  matrix products  29.8 us (8%)
  other arithmetic  17.7 us (5%)
  between operations  14 us (4%)
  starting transfers between devices  11.3 us (3%)
    unnamed x1, blocking collectives  66 us
    all_to_all x1, blocking collectives, body(): lax.all_to_all(packed.reshape(experts_total, capacity, width_here), 'ctx'...  51.8 us
    psum x1, waiting for transfers between devices, body(): lax.psum(partial_out.astype(jnp.bfloat16), 'head').astype(jnp.float32)  51.4 us
    unnamed x5, waiting for transfers between devices  38.2 us
    all_gather x1, waiting for transfers between devices, body(): lax.all_gather(out_weight, 'ctx', axis=1, tiled=True)  23.6 us
    unnamed x34, local copies, waits for them, and re-layouts  12.5 us
    all_to_all x1, starting transfers between devices, body(): lax.all_to_all(summed.reshape(experts_total, capacity, slice_width), 'ctx...  11 us
    dot_general x1, matrix products, body(): jnp.dot(hidden, w_down[0], preferred_element_type=jnp.float32)  9.52 us
  transfers between devices with their start and end apart: 5, of which 4 were waited for; matrix products, arithmetic and copies ran while one was open for 11% of the time, Pallas kernels for 0%

commit v1 on v0

--- a/solution.py
+++ b/solution.py
@@ -93,11 +93,10 @@
         .transpose(1, 0, 2)
         .reshape(token_count, heads_here * head_size)
     )
-    partial_out = jnp.dot(
-        heads_normed,
-        lax.all_gather(out_weight, "ctx", axis=1, tiled=True),
-        preferred_element_type=jnp.float32,
+    lift_points = lambda v0: jnp.concatenate(
+        lax.all_to_all(jnp.stack(lax.axis_size("ctx") * [v0]), "ctx", 0, 0), axis=1
     )
+    partial_out = jnp.dot(heads_normed, lift_points(out_weight), preferred_element_type=jnp.float32)
     model_width = residual.shape[1]
     experts_total = router.shape[1]
     capacity = 2 * token_count * TOP // experts_total

time: 358 us -> 373 us (1.042)
  blocking collectives: 118 us -> 145 us
  waiting for transfers between devices: 121 us -> 97.1 us
  starting transfers between devices: 11.3 us -> 19.6 us
    unnamed x1, blocking collectives: 66 us -> 93.4 us
    all_gather x1 -> x0, waiting for transfers between devices: 23.6 us -> none  [body(): lax.all_gather(out_weight, 'ctx', axis=1, tiled=True)]
    all_to_all x0 -> x1, starting transfers between devices: none -> 8.76 us  [body(): lax.all_to_all(jnp.stack(lax.axis_size('ctx') * [v0]), 'ctx', 0, 0)]
    unnamed x34 -> x36, local copies, waits for them, and re-layouts: 12.5 us -> 11.9 us
    unnamed x5 -> x4, waiting for transfers between devices: 38.2 us -> 37.7 us
  transfers between devices with their start and end apart: 5 -> 5, of which waited for: 4 -> 3; matrix products, arithmetic and copies ran while one was open for 11% -> 11% of each run, Pallas kernels for 0% -> 0%
where the time goes in v1:
time: 373 us; the launch traced here: 371 us
  blocking collectives  145 us (39%)
  waiting for transfers between devices  97.1 us (26%)
  local copies, waits for them, and re-layouts  47.8 us (13%)
  matrix products  29.8 us (8%)
  starting transfers between devices  19.6 us (5%)
  other arithmetic  17.7 us (5%)
  between operations  14 us (4%)
    unnamed x1, blocking collectives  93.4 us
    psum x1, waiting for transfers between devices, body(): lax.psum(partial_out.astype(jnp.bfloat16), 'head').astype(jnp.float32)  52 us
    all_to_all x1, blocking collectives, body(): lax.all_to_all(packed.reshape(experts_total, capacity, width_here), 'ctx'...  51.8 us
    unnamed x4, waiting for transfers between devices  37.7 us
    unnamed x36, local copies, waits for them, and re-layouts  11.9 us
    all_to_all x1, starting transfers between devices, body(): lax.all_to_all(summed.reshape(experts_total, capacity, slice_width), 'ctx...  10.6 us
    dot_general x1, matrix products, body(): jnp.dot(hidden, w_down[0], preferred_element_type=jnp.float32)  9.52 us
    all_to_all x1, starting transfers between devices, body(): lax.all_to_all(jnp.stack(lax.axis_size('ctx') * [v0]), 'ctx', 0, 0)  8.76 us
  transfers between devices with their start and end apart: 5, of which 3 were waited for; matrix products, arithmetic and copies ran while one was open for 11% of the time, Pallas kernels for 0%

profile of v1, /device:TPU:1, one launch (start us, length us, event | category | flops | bytes accessed | tf_op | source)
XLA Modules:
  0.0 371.2 jit_solution(14964918147618845600)
XLA Ops:
  6.5 1.1 reduce_window_sum.26
  7.7 0.2 slice_reduce_fusion.1
  7.9 0.6 exponential_bitcast_fusion
  8.5 1.7 copy.79
  10.1 1.9 convolution_convert_fusion.2
  12.0 0.0 all-gather.4.cloned.1.call-update
  12.0 3.0 stack.2
  15.0 8.8 %all-to-all-start = ((bf16[32,512,96]{1,2,0:T(8,128)(2,1)}), bf16[32,512,96]{1,2,0:T(8,128)(2,1)}, u32[]{:S(2)}, u32[]{:S(2)}) async-start(bf16[32,512,96]{1,2,0:T(8,128)(2,1)} %stack.2), calls=%async_computation | async-start | bytes 6291456 | tf_op jit(solution)/shard_map/all_to_all | solution.py:97
  23.8 0.0 all-reduce.3.cloned.1.call-start
  23.8 0.6 dynamic-slice
  25.1 0.2 dynamic-update-slice
  25.3 93.4 %all-reduce = f32[128]{0:T(128)} all-reduce(f32[128]{0:T(128)S(1)} %dynamic-update-slice), channel_id=2, replica_groups=mesh['ctx'=32,'head'=8] {'ctx'}, use_global_device_ids=true, to_apply=%add | all-reduce | flops 128 | bytes 1024
  118.7 0.7 reshape.198
  119.5 0.7 copy.66
  120.1 1.4 copy.67
  121.5 1.6 eq.39
  123.1 0.8 select_reduce_fusion
  123.9 1.9 convolution_multiply_fusion
  125.8 0.0 copy-start.11
  125.8 5.7 %fusion = f32[4,1,128,128]{3,1,2,0:T(1,128)S(1)} fusion(f32[32,4,1,1]{0,2,3,1:T(1,128)S(1)} %bitcast.154, bf16[32,4,128,128]{3,2,1,0:T(8,128)(2,1)} %bitcast.145), kind=kOutput, calls=%fused_computation.3 | convolution fusion | flops 25165824 | bytes 4456960 | tf_op jit(solution)/shard_map/jh,jhde->hde/dot_general | solution.py:20
  131.6 0.4 fusion.39
  132.0 0.4 fusion.26
  132.5 0.8 fusion.30
  133.3 4.0 %convolution_convert_fusion.1 = bf16[128,3072]{1,0:T(8,128)(2,1)} fusion(bf16[128,512]{0,1:T(8,128)(2,1)} %bitcast.150, bf16[512,3072]{0,1:T(8,128)(2,1)} %bitcast.20), kind=kOutput, calls=%fused_computation.5 | convolution fusion | flops 403046400 | bytes 4063232 | tf_op jit(solution)/shard_map/dot_general | solution.py:99
  137.3 0.0 all-reduce.3.cloned.1.call-update
  137.3 0.2 reduce-scatter.4.cloned.1.call-start
  137.5 1.3 fusion.48
  138.8 1.5 eq.35
  140.4 1.9 reduce-window.6
  142.3 1.5 slice_reduce_fusion
  143.8 1.3 reduce-window.9
  145.0 0.7 slice.28
  145.7 1.4 fusion.47
  147.1 1.4 reshape.174
  148.6 1.5 copy.70
  150.1 1.2 multiply_add_fusion
  151.3 1.4 copy.71
  152.7 1.5 reshape.175
  154.2 1.2 compare_select_fusion
  155.4 52.0 %all-reduce.3.cloned.1.call-done = bf16[128,3072]{1,0:T(8,128)(2,1)} async-done(((bf16[128,3072]{1,0:T(8,128)(2,1)}), bf16[128,3072]{1,0:T(8,128)(2,1)}) %all-reduce.3.cloned.1.call-update) | async-done | bytes 786448 | tf_op jit(solution)/shard_map/psum | solution.py:105
  207.4 2.7 fusion.51
  210.1 0.2 multiply_reduce_fusion
  210.4 0.7 copy-done.1
  211.1 0.5 copy-done.12
  211.6 0.2 multiply_convert_fusion
  211.8 2.0 broadcast_in_dim.93
  213.8 4.6 %reshape.194 = bf16[256,3072]{1,0:T(8,128)(2,1)} reshape(bf16[128,2,3072]{2,1,0:T(2,128)(2,1)} %broadcast_in_dim.93) | data formatting | bytes 3145728 | tf_op jit(solution)/shard_map/reshape | solution.py:116
  218.4 5.8 %scatter_custom_fusion = bf16[512,3072]{1,0:T(8,128)(2,1)} fusion(s32[256]{0:T(256)} %bitcast.155, bf16[256,3072]{1,0:T(8,128)(2,1)} %reshape.194, bf16[]{:T(256)} %constant.42.clone.1), kind=kCustom, calls=%fused_computation.12 | custom fusion | bytes 3146240 | tf_op jit(solution)/shard_map/scatter | solution.py:117
  224.2 51.8 %all_to_all.15 = bf16[32,16,3072]{2,1,0:T(8,128)(2,1)S(1)} all-to-all(bf16[32,16,3072]{2,1,0:T(8,128)(2,1)} %bitcast.144), channel_id=1, replica_groups=mesh['ctx'=32,'head'=8] {'ctx'}, dimensions={0} | all-to-all | bytes 6291456 | tf_op jit(solution)/shard_map/all_to_all | solution.py:118
  276.0 1.7 copy-done.2
  277.7 3.2 fusion.5
  280.8 9.5 %convolution_convert_fusion = bf16[512,3072]{1,0:T(8,128)(2,1)} fusion(bf16[1,576,3072]{2,1,0:T(8,128)(2,1)S(1)} %copy-done, bf16[512,3072]{1,0:T(8,128)(2,1)} %bitcast.147, bf16[1,3072,576]{1,2,0:T(8,128)(2,1)} %param.23, f32[512,576]{0,1:T(8,128)} %fusion.5), kind=kOutput, calls=%fused_computation.2 | convolution fusion | flops 3627220992 | bytes 14548992 | tf_op jit(solution)/shard_map/dot_general | solution.py:129
  290.3 4.7 %copy.82 = bf16[512,3072]{0,1:T(8,128)(2,1)} copy(bf16[512,3072]{1,0:T(8,128)(2,1)} %convolution_convert_fusion) | data formatting | bytes 6291456
  295.0 0.0 reduce-scatter.4.cloned.1.call-update
  295.1 1.2 pad_clamp_fusion
  296.3 37.6 %reduce-scatter.4.cloned.1.call-done = bf16[384,512]{1,0:T(8,128)(2,1)} async-done(((bf16[3072,512]{1,0:T(8,128)(2,1)}), bf16[384,512]{1,0:T(8,128)(2,1)}) %reduce-scatter.4.cloned.1.call-update) | async-done | bytes 393232
  333.9 2.0 copy.83
  335.9 10.6 %all-to-all-start.2 = ((bf16[32,16,384]{2,1,0:T(8,128)(2,1)}), bf16[32,16,384]{2,1,0:T(8,128)(2,1)}, u32[]{:S(2)}, u32[]{:S(2)}) async-start(bf16[32,16,384]{2,1,0:T(8,128)(2,1)} %bitcast.148), calls=%async_computation.2 | async-start | bytes 786432 | tf_op jit(solution)/shard_map/all_to_all | solution.py:133
  346.4 2.8 fusion.18
  349.3 7.4 %all-to-all-done.2 = bf16[32,16,384]{2,1,0:T(8,128)(2,1)} async-done(((bf16[32,16,384]{2,1,0:T(8,128)(2,1)}), bf16[32,16,384]{2,1,0:T(8,128)(2,1)}, u32[]{:S(2)}, u32[]{:S(2)}) %all-to-all-start.2) | async-done | bytes 393248 | tf_op jit(solution)/shard_map/all_to_all | solution.py:133
  356.6 3.0 gather_fusion
  359.6 1.9 reshape.181
  361.5 1.5 fusion.52
  362.9 1.7 fusion.35
  (38 shorter events, 0.1 us)
Async XLA Ops:
  6.5 274.3 %copy-start = (bf16[1,576,3072]{2,1,0:T(8,128)(2,1)S(1)}, bf16[1,576,3072]{2,1,0:T(8,128)(2,1)}, u32[]{:S(2)}) copy-start(bf16[1,576,3072]{2,1,0:T(8,128)(2,1)} %param.24) | copy-start | bytes 10616836
  6.5 119.3 %all-gather.4.cloned.1.call-start = ((), (), s32[]{:S(2)}) async-start(), calls=%async_computation.5 | async-start | bytes 4325376 | tf_op jit(solution)/shard_map/all_gather | solution.py:13
  7.7 7.3 %copy-start.7 = (f32[4,128]{1,0:T(4,128)}, f32[4,128]{1,0:T(4,128)S(1)}, u32[]{:S(2)}) copy-start(f32[4,128]{1,0:T(4,128)S(1)} %reduce_window_sum.26) | copy-start | bytes 6148
  15.0 8.8 %copy-start.14 = (u32[256]{0:T(256)S(1)}, u32[256]{0:T(256)}, u32[]{:S(2)}) copy-start(u32[256]{0:T(256)} %constant.51) | copy-start | bytes 3076
  15.0 118.3 %all-to-all-start = ((bf16[32,512,96]{1,2,0:T(8,128)(2,1)}), bf16[32,512,96]{1,2,0:T(8,128)(2,1)}, u32[]{:S(2)}, u32[]{:S(2)}) async-start(bf16[32,512,96]{1,2,0:T(8,128)(2,1)} %stack.2), calls=%async_computation | async-start | bytes 6291456 | tf_op jit(solution)/shard_map/all_to_all | solution.py:97
  23.8 183.6 %all-reduce.3.cloned.1.call-start = ((), (), s32[]{:S(2)}) async-start(), calls=%async_computation.4 | async-start | bytes 1572864 | tf_op jit(solution)/shard_map/psum | solution.py:105
  120.1 11.9 %copy-start.10 = (f32[4,128]{1,0:T(4,128)S(1)}, f32[4,128]{1,0:T(4,128)}, u32[]{:S(2)}) copy-start(f32[4,128]{1,0:T(4,128)} %get-tuple-element.12) | copy-start | bytes 6148
  125.8 6.7 %copy-start.9 = (f32[128,4]{0,1:T(4,128)S(1)}, f32[128,4]{0,1:T(4,128)}, u32[]{:S(2)}) copy-start(f32[128,4]{0,1:T(4,128)} %get-tuple-element.11) | copy-start | bytes 6148
  125.8 5.8 %copy-start.5 = (bf16[128,512]{1,0:T(8,128)(2,1)S(1)}, bf16[128,512]{1,0:T(8,128)(2,1)}, u32[]{:S(2)}) copy-start(bf16[128,512]{1,0:T(8,128)(2,1)} %param.13) | copy-start | bytes 393220
  125.8 6.2 %copy-start.3 = (bf16[128,512]{1,0:T(8,128)(2,1)S(1)}, bf16[128,512]{1,0:T(8,128)(2,1)}, u32[]{:S(2)}) copy-start(bf16[128,512]{1,0:T(8,128)(2,1)} %param.15) | copy-start | bytes 393220
  125.8 6.2 %copy-start.4 = (f32[4,128,128]{2,1,0:T(8,128)S(1)}, f32[4,128,128]{2,1,0:T(8,128)}, u32[]{:S(2)}) copy-start(f32[4,128,128]{2,1,0:T(8,128)} %convolution_multiply_fusion) | copy-start | bytes 786436
  125.8 6.7 %copy-start.11 = (f32[512]{0:T(512)S(1)}, f32[512]{0:T(512)}, u32[]{:S(2)}) copy-start(f32[512]{0:T(512)} %param.19) | copy-start | bytes 6148
  132.4 17.6 %copy-start.8 = (s32[128,2]{0,1:T(2,128)S(1)}, s32[128,2]{0,1:T(2,128)}, u32[]{:S(2)}) copy-start(s32[128,2]{0,1:T(2,128)} %param.25) | copy-start | bytes 3076
  137.3 74.3 %copy-start.6 = (f32[3072]{0:T(1024)S(1)}, f32[3072]{0:T(1024)}, u32[]{:S(2)}) copy-start(f32[3072]{0:T(1024)} %param.20) | copy-start | bytes 36868
  137.3 196.6 %reduce-scatter.4.cloned.1.call-start = ((), (), s32[]{:S(2)}) async-start(), calls=%async_computation.6 | async-start | bytes 3538944
  210.1 0.9 copy-start.1
  211.1 0.5 copy-start.12
  224.2 53.5 %copy-start.13 = (bf16[1,3072,576]{1,2,0:T(8,128)(2,1)S(1)}, bf16[1,3072,576]{1,2,0:T(8,128)(2,1)}, u32[]{:S(2)}) copy-start(bf16[1,3072,576]{1,2,0:T(8,128)(2,1)} %param.22) | copy-start | bytes 10616836
  276.0 1.7 copy-start.2
  335.9 20.8 %all-to-all-start.2 = ((bf16[32,16,384]{2,1,0:T(8,128)(2,1)}), bf16[32,16,384]{2,1,0:T(8,128)(2,1)}, u32[]{:S(2)}, u32[]{:S(2)}) async-start(bf16[32,16,384]{2,1,0:T(8,128)(2,1)} %bitcast.148), calls=%async_computation.2 | async-start | bytes 786432 | tf_op jit(solution)/shard_map/all_to_all | solution.py:133
Sparse Core Ops, SparseCore 0:
  12.2 78.7 all-gather.3
  137.4 69.9 all-reduce.2
  295.2 38.6 reduce-scatter.3
